TPU v7x, 128 devices: a whole 4x4x4 slice. The times are simulated.
128 devices in a mesh: row: 8 (over x, core), col: 16 (over z, y).
Axes of the slice: x: 4, y: 4, z: 4, core: 2. Of those that a mesh axis runs over, the one named last changes fastest.
Arguments:
- unit_factor: float32 [4, 1024, 2, 2048], P(None, 'row', None, 'col'), may hold values from -0.125 to 0.125
- pivot_inverse: float32 [4, 1024, 2, 2048], P(None, 'row', None, 'col')
- supernode: int32 [32], replicated, may hold values from 0 to 2, never falling along the last dimension, each value on 1 to 16 neighbouring positions
- row_bits: int32 [32, 2], replicated, may hold values 0 or 1
Outputs:
- inverse_blocks: float32 [4, 1024, 2, 2048], P(None, 'row', None, 'col')
Inputs may be any that keep to these rules, and one draw needn't show every extreme that they name: The supernode index never decreases from one block to the next; each supernode has 1 to 16 blocks, one of them exactly 16.
All inputs are finite; a program needn't handle non-finite values.
Results may differ from a plain program's by a relative error of at most 0.0001.
Values sent between devices are 32-bit elements; how exact they have to be, the bound alone decides.
No kernel may reach another device: no remote copies, remote signals or barrier semaphores. Data moves between devices by JAX's collectives and lax.ppermute only.
A program may use at most 128 MiB of HBM per device.

v0:
```python
import jax
import jax.numpy as jnp
from jax import lax
from jax.sharding import PartitionSpec as P

SUPERNODES = 3


def pick(table, index):
    hits = index[:, None] == jnp.arange(table.shape[0])[None, :]
    return jnp.sum(jnp.where(hits, table[None, :], 0.0), axis=1)


def shards(unit_factor, pivot_inverse, supernode, row_bits):
    n_row = lax.axis_size("row")
    n_col = lax.axis_size("col")
    brows, width, bcols, _ = unit_factor.shape
    whole = brows * n_row * width
    row_ids = jnp.arange(brows) * n_row + lax.axis_index("row")
    col_ids = jnp.arange(bcols) * n_col + lax.axis_index("col")
    highest = lax.Precision.HIGHEST

    def member_of(level):
        return (supernode == level).astype(jnp.float32)

    def local_mask(for_rows, for_cols):
        return (
            pick(for_rows, row_ids)[:, None, None, None]
            * pick(for_cols, col_ids)[None, None, :, None]
        )

    last = SUPERNODES - 1
    inverse = pivot_inverse * local_mask(member_of(last), member_of(last))
    column_panel = lax.all_gather(unit_factor, "row", axis=1, tiled=True).reshape(
        whole, bcols * width
    )
    row_panel = lax.all_gather(unit_factor, "col", axis=3, tiled=True).reshape(brows * width, whole)
    for level in range(last - 1, -1, -1):
        member = member_of(level)
        inside = jnp.logical_and(supernode > level, jnp.all(row_bits[:, level:] == 1, axis=1))
        struct = inside.astype(jnp.float32)
        ancestors = inverse * local_mask(struct, struct)
        ucols = (
            column_panel
            * jnp.repeat(struct, width)[:, None]
            * jnp.repeat(pick(member, col_ids), width)[None, :]
        )
        urows = (
            row_panel
            * jnp.repeat(pick(struct, row_ids), width)[:, None]
            * jnp.repeat(member, width)[None, :]
        )
        stacked = ucols.reshape(bcols, n_col * width, bcols * width)
        spread = urows.reshape(brows * width, brows, n_row * width)
        flat_ancestors = ancestors.reshape(brows * width, bcols * width)
        image = jnp.einsum(
            "kajp,jpl->kal",
            lax.all_gather(ancestors, "col", axis=3, tiled=True),
            stacked,
            precision=highest,
            preferred_element_type=jnp.float32,
        )
        flat_image = image.reshape(brows * width, bcols * width)
        update = lax.psum_scatter(
            jnp.einsum(
                "hkp,hl->pkl",
                spread,
                flat_image - flat_ancestors,
                precision=highest,
                preferred_element_type=jnp.float32,
            ),
            "row",
            scatter_dimension=0,
            tiled=True,
        )
        update = jnp.transpose(update, (1, 0, 2)).reshape(brows, width, bcols, width)
        inverse = (
            inverse
            - image.reshape(brows, width, bcols, width)
            + update
            + pivot_inverse * local_mask(member, member)
        )
    return inverse


def solution(mesh):
    in_specs = (P(None, "row", None, "col"), P(None, "row", None, "col"), P(), P())
    out_specs = P(None, "row", None, "col")
    return jax.shard_map(shards, mesh=mesh, in_specs=in_specs, out_specs=out_specs, check_vma=False)
```

profile of v0, /device:TPU:0, one launch (start us, length us, event | category | flops | bytes accessed | tf_op | source)
XLA Modules:
  0.0 454.2 jit_solution(7438462885738137960)
XLA Ops:
  6.5 0.7 all-gather.7.cloned.1.call-update
  7.3 0.7 all-gather.9.cloned.1.call-update
  8.1 0.7 compare_reduce_fusion
  8.8 0.7 compare_convert_fusion.2
  9.5 0.2 select_reduce_fusion
  9.7 0.3 select_reduce_fusion.5
  10.1 2.0 multiply_multiply_fusion.2
  12.1 1.2 copy.34
  13.6 0.2 copy.35
  14.1 29.4 %all-gather.7.cloned.1.call-done = f32[4,1024,2,128]{3,2,1,0:T(2,128)} async-done(((f32[4,128,2,128]{3,2,1,0:T(2,128)}), f32[4,1024,2,128]{3,2,1,0:T(2,128)}) %all-gather.7.cloned.1.call-update) | async-done | bytes 4194320 | tf_op jit(solution)/shard_map/all_gather | solution.py:34
  43.6 6.5 %reshape.289 = f32[2,2048,256]{2,1,0:T(8,128)} reshape(f32[4,1024,2,128]{3,2,1,0:T(2,128)} %all-gather.7.cloned.1.call-done) | data formatting | bytes 8388608 | tf_op jit(solution)/shard_map/reshape | solution.py:34
  50.0 113.4 %all-gather.9.cloned.1.call-done = f32[4,128,2,2048]{3,2,1,0:T(2,128)} async-done(((f32[4,128,2,128]{3,2,1,0:T(2,128)}), f32[4,128,2,2048]{3,2,1,0:T(2,128)}) %all-gather.9.cloned.1.call-update) | async-done | bytes 8388624 | tf_op jit(solution)/shard_map/all_gather | solution.py:37
  163.4 10.5 %multiply_multiply_fusion = (f32[4,128,2,2048]{3,2,1,0:T(2,128)}, f32[4,128,2,2048]{3,2,1,0:T(2,128)}) fusion(f32[4,128,2,2048]{3,2,1,0:T(2,128)} %all-gather.9.cloned.1.call-done, f32[4]{0:T(128)S(1)} %get-tuple-element.6, f32[2,2048]{1,0:T(2,128)S(1)} %mul.288, f32[2,2048]{1,0:T(2,128)S(1)} %mul.267, f32[4]{0:T(128)S(1)} %get-tuple-element.8), kind=kLoop, calls=%fused_computation.4 | loop fusion | flops 8388608 | bytes 25198624 | tf_op jit(solution)/shard_map/mul | solution.py:49
  173.9 12.4 %mul.270 = f32[512,4,1024]{2,1,0:T(4,128)} reshape(f32[4,128,2,2048]{3,2,1,0:T(2,128)} %get-tuple-element.16) | data formatting | bytes 16777216 | tf_op jit(solution)/shard_map/mul | solution.py:49
  186.4 57.4 %all-gather.5.cloned.1.call-done = f32[4,128,2,2048]{3,1,2,0:T(8,128)} async-done(((f32[4,128,2,128]{3,1,2,0:T(8,128)}), f32[4,128,2,2048]{3,1,2,0:T(8,128)}) %all-gather.5.cloned.1.call-update) | async-done | bytes 8388624 | tf_op jit(solution)/shard_map/all_gather | solution.py:58
  243.8 11.4 %fusion.29 = (f32[4,128,256]{2,1,0:T(8,128)S(1)}, f32[4,128,256]{2,1,0:T(8,128)S(1)}) fusion(f32[4,128,256]{2,1,0:T(8,128)S(1)} %copy.35, f32[4,128,2,2048]{3,1,2,0:T(8,128)} %all-gather.5.cloned.1.call-done, f32[2,2048,256]{2,1,0:T(8,128)} %reshape.289, f32[256]{0:T(256)S(1)} %broadcast_bitcast_fusion.3, f32[2,2048]{1,0:T(2,128)S(1)} %bitcast.70), kind=kOutput, calls=%fused_computation.58 | convolution fusion | flops 6444679168 | bytes 14173184 | tf_op jit(solution)/shard_map/kajp,jpl->kal/dot_general | solution.py:56
  255.2 12.4 %fusion.12 = f32[1024,4,256]{0,2,1:T(8,128)} fusion(f32[512,256,1]{1,0,2:T(8,128)S(1)} %bitcast.63, f32[512,4,1024]{2,1,0:T(4,128)S(1)} %copy-done.1), kind=kOutput, calls=%fused_computation.14 | convolution fusion | flops 6442450944 | bytes 13107200 | tf_op jit(solution)/shard_map/hkp,hl->pkl/dot_general | solution.py:65
  268.0 0.2 copy.33
  268.2 36.7 %reduce-scatter.3.cloned.1.call-done = f32[128,4,256]{0,2,1:T(8,128)} async-done(((f32[1024,4,256]{0,2,1:T(8,128)}), f32[128,4,256]{0,2,1:T(8,128)}) %reduce-scatter.3.cloned.1.call-update) | async-done | bytes 524304 | tf_op jit(solution)/shard_map/reduce_scatter | solution.py:64
  304.9 1.2 copy.38
  306.2 1.0 broadcast_multiply_fusion
  307.5 12.6 %mul.291 = f32[512,4,1024]{2,1,0:T(4,128)} reshape(f32[4,128,2,2048]{3,2,1,0:T(2,128)} %get-tuple-element.15) | data formatting | bytes 16777216 | tf_op jit(solution)/shard_map/mul | solution.py:49
  320.1 0.2 copy.42
  320.3 0.2 copy.43
  320.5 63.2 %all-gather.11.cloned.1.call-done = f32[4,128,2,2048]{3,1,2,0:T(8,128)} async-done(((f32[4,128,2,128]{3,1,2,0:T(8,128)}), f32[4,128,2,2048]{3,1,2,0:T(8,128)}) %all-gather.11.cloned.1.call-update) | async-done | bytes 8388624 | tf_op jit(solution)/shard_map/all_gather | solution.py:58
  383.7 11.4 %fusion.30 = (f32[4,128,256]{2,1,0:T(8,128)S(1)}, f32[4,128,256]{2,1,0:T(8,128)S(1)}) fusion(f32[4,128,256]{2,1,0:T(8,128)S(1)} %copy.43, f32[4,128,2,2048]{3,1,2,0:T(8,128)} %all-gather.11.cloned.1.call-done, f32[2,2048,256]{2,1,0:T(8,128)} %reshape.289, f32[256]{0:T(256)S(1)} %broadcast_bitcast_fusion.2, f32[2,2048]{1,0:T(2,128)S(1)} %bitcast.71), kind=kOutput, calls=%fused_computation.59 | convolution fusion | flops 6444679168 | bytes 14173184 | tf_op jit(solution)/shard_map/kajp,jpl->kal/dot_general | solution.py:56
  395.1 12.2 %fusion.15 = f32[1024,4,256]{0,2,1:T(8,128)} fusion(f32[512,256,1]{1,0,2:T(8,128)S(1)} %bitcast.62, f32[512,4,1024]{2,1,0:T(4,128)S(1)} %copy-done), kind=kOutput, calls=%fused_computation.15 | convolution fusion | flops 6442450944 | bytes 13107200 | tf_op jit(solution)/shard_map/hkp,hl->pkl/dot_general | solution.py:65
  407.7 0.2 copy.41
  407.9 36.8 %reduce-scatter.5.cloned.1.call-done = f32[128,4,256]{0,2,1:T(8,128)} async-done(((f32[1024,4,256]{0,2,1:T(8,128)}), f32[128,4,256]{0,2,1:T(8,128)}) %reduce-scatter.5.cloned.1.call-update) | async-done | bytes 524304 | tf_op jit(solution)/shard_map/reduce_scatter | solution.py:64
  444.6 1.2 copy.46
  445.9 0.3 multiply_add_fusion
  446.2 1.2 copy.48
  (39 shorter events, 1.7 us)
Async XLA Ops:
  6.5 37.0 %all-gather.7.cloned.1.call-start = ((), (), s32[]{:S(2)}) async-start(), calls=%async_computation.3 | async-start | bytes 4718592 | tf_op jit(solution)/shard_map/all_gather | solution.py:34
  7.3 156.2 %all-gather.9.cloned.1.call-start = ((), (), s32[]{:S(2)}) async-start(), calls=%async_computation.4 | async-start | bytes 8912896 | tf_op jit(solution)/shard_map/all_gather | solution.py:37
  8.0 235.8 %all-gather.5.cloned.1.call-start = ((), (), s32[]{:S(2)}) async-start(), calls=%async_computation.2 | async-start | bytes 8912896 | tf_op jit(solution)/shard_map/all_gather | solution.py:58
  12.0 292.9 %reduce-scatter.3.cloned.1.call-start = ((), (), s32[]{:S(2)}) async-start(), calls=%async_computation.5 | async-start | bytes 4718592 | tf_op jit(solution)/shard_map/reduce_scatter | solution.py:64
  243.8 11.5 %copy-start.1 = (f32[512,4,1024]{2,1,0:T(4,128)S(1)}, f32[512,4,1024]{2,1,0:T(4,128)}, u32[]{:S(2)}) copy-start(f32[512,4,1024]{2,1,0:T(4,128)} %mul.270) | copy-start | bytes 25165828
  255.2 50.9 %copy-start.3 = (f32[4,128,2,128]{3,2,1,0:T(2,128)S(1)}, f32[4,128,2,128]{3,2,1,0:T(2,128)}, u32[]{:S(2)}) copy-start(f32[4,128,2,128]{3,2,1,0:T(2,128)} %param.5) | copy-start | bytes 1572868
  267.7 116.0 %all-gather.11.cloned.1.call-start = ((), (), s32[]{:S(2)}) async-start(), calls=%async_computation.6 | async-start | bytes 8912896 | tf_op jit(solution)/shard_map/all_gather | solution.py:58
  307.2 137.4 %reduce-scatter.5.cloned.1.call-start = ((), (), s32[]{:S(2)}) async-start(), calls=%async_computation.7 | async-start | bytes 4718592 | tf_op jit(solution)/shard_map/reduce_scatter | solution.py:64
  307.5 12.6 %copy-start.2 = (f32[4,128,2,128]{3,1,2,0:T(8,128)S(1)}, f32[4,128,2,128]{3,1,2,0:T(8,128)}, u32[]{:S(2)}) copy-start(f32[4,128,2,128]{3,1,2,0:T(8,128)} %broadcast_multiply_fusion) | copy-start | bytes 1572868
  383.7 11.4 %copy-start = (f32[512,4,1024]{2,1,0:T(4,128)S(1)}, f32[512,4,1024]{2,1,0:T(4,128)}, u32[]{:S(2)}) copy-start(f32[512,4,1024]{2,1,0:T(4,128)} %mul.291) | copy-start | bytes 25165828
Sparse Core Ops, SparseCore 0:
  9.0 34.4 all-gather.6
  45.7 117.7 all-gather.8
  165.6 78.1 all-gather.4
  267.8 37.0 reduce-scatter.2
  307.3 76.3 all-gather.10
  407.5 37.0 reduce-scatter.4
where the time goes:
time: 455 us; the launch traced here: 454 us
  waiting for transfers between devices  338 us (74%)
  matrix products  47.5 us (10%)
  local copies, waits for them, and re-layouts  38.6 us (8%)
  other arithmetic  15.9 us (3%)
  between operations  13.6 us (3%)
    all_gather x2, waiting for transfers between devices, shards(): lax.all_gather(ancestors, 'col', axis=3, tiled=True)  121 us
    all_gather x1, waiting for transfers between devices, shards(): lax.all_gather(unit_factor, 'col', axis=3, tiled=True)  113 us
    reduce_scatter x2, waiting for transfers between devices, shards(): lax.psum_scatter(jnp.einsum('hkp,hl->pkl', spread, flat_image - flat_ance...  73.5 us
    all_gather x1, waiting for transfers between devices, shards(): lax.all_gather(unit_factor, 'row', axis=1, tiled=True)  29.4 us
    mul x4, local copies, waits for them, and re-layouts, shards(): row_panel * jnp.repeat(pick(struct, row_ids), width)[:, None]  25.1 us
    dot_general x2, matrix products, shards(): jnp.einsum('hkp,hl->pkl', spread, flat_image - flat_ancestors, precision=...  24.6 us
    dot_general x2, matrix products, shards(): jnp.einsum('kajp,jpl->kal', lax.all_gather(ancestors, 'col', axis=3, tile...  22.9 us
    mul x1, other arithmetic, shards(): row_panel * jnp.repeat(pick(struct, row_ids), width)[:, None]  10.5 us
  transfers between devices with their start and end apart: 6, of which 6 were waited for; matrix products, arithmetic and copies ran while one was open for 11% of the time, Pallas kernels for 0%

commit v1 on v0

v1 whole, which is shorter than its diff:
```python
import jax
import jax.numpy as jnp
from jax import lax
from jax.sharding import PartitionSpec as P

SUPERNODES = 3
HIGHEST = lax.Precision.HIGHEST


def dot(spec, a, b):
    return jnp.einsum(spec, a, b, precision=HIGHEST, preferred_element_type=jnp.float32)


def shards(unit_factor, pivot_inverse, supernode, row_bits):
    n_row = lax.axis_size("row")
    n_col = lax.axis_size("col")
    brows, width, bcols, _ = unit_factor.shape
    nb = brows * n_row
    r = lax.axis_index("row")
    q = lax.axis_index("col")

    def rows_of(v):
        return lax.dynamic_index_in_dim(v.reshape(brows, n_row), r, axis=1, keepdims=False)

    def cols_of(v):
        return lax.dynamic_index_in_dim(v.reshape(bcols, n_col), q, axis=1, keepdims=False)

    def mask(a, rm=None, cm=None):
        if rm is not None:
            a = a * rm[:, None, None, None]
        if cm is not None:
            a = a * cm[None, None, :, None]
        return a

    def pack_rows(a):
        return a.reshape((brows // 2, 2) + a.shape[1:]).sum(axis=0)

    def unpack_rows(a, rm):
        full = jnp.concatenate([a] * (brows // 2), axis=0)
        return full * rm.reshape((brows,) + (1,) * (a.ndim - 1))

    def scatter_rows(zp):
        zp = jnp.swapaxes(zp.reshape(n_col // n_row, n_row, width, bcols * width), 0, 1)
        zp = zp.reshape(n_col * width, bcols * width)
        zr = lax.psum_scatter(zp, "row", scatter_dimension=0, tiled=True)
        return zr.reshape(n_col // n_row, width, bcols, width)

    f32 = jnp.float32
    member = [(supernode == s).astype(f32) for s in range(SUPERNODES)]
    struct = [
        jnp.logical_and(supernode > s, jnp.all(row_bits[:, s:] == 1, axis=1)).astype(f32)
        for s in range(SUPERNODES - 1)
    ]

    last = SUPERNODES - 1
    rM2, cM2 = rows_of(member[last]), cols_of(member[last])
    x = mask(pivot_inverse, rM2, cM2)

    S, M = struct[1], member[1]
    rS, cS, rM, cM = rows_of(S), cols_of(S), rows_of(M), cols_of(M)
    xm = mask(x, rS, cS)
    xc = pack_rows(xm.sum(axis=2))
    uc = pack_rows(mask(unit_factor, rS, cM).sum(axis=2))
    xg = lax.all_gather(xc, "col")
    ucol = lax.all_gather(uc, "row")
    urow = lax.all_gather(uc, "col")
    xfull = jnp.transpose(xg, (1, 2, 0, 3))[:, :, None] * S.reshape(bcols, n_col)[None, None, :, :, None]
    xfull = xfull.reshape(2, width, nb, width)
    ufull = jnp.concatenate([jnp.transpose(ucol, (1, 0, 2, 3))] * (brows // 2), axis=0)
    ufull = (ufull * S.reshape(brows, n_row)[:, :, None, None]).reshape(nb, width, width)
    y = dot("pakx,kxb->pab", xfull, ufull)
    yl = mask(unpack_rows(y, rS)[:, :, None, :], None, cM)
    x = x - yl
    wc = pack_rows(yl - xm)
    zp = dot("qpax,pacb->qxcb", urow, wc)
    x = x + unpack_rows(scatter_rows(zp), rM) + mask(pivot_inverse, rM, cM)

    S, M = struct[0], member[0]
    rS, cS, rM, cM = rows_of(S), cols_of(S), rows_of(M), cols_of(M)
    xm = mask(x, rS, cS)
    uc = mask(unit_factor, rS, cM).sum(axis=2)
    ucol = lax.all_gather(uc, "row")
    urow = lax.all_gather(uc, "col")
    xg = lax.all_gather(xm, "col")
    xfull = jnp.transpose(xg, (1, 2, 3, 0, 4)).reshape(brows, width, nb, width)
    ufull = jnp.transpose(ucol, (1, 0, 2, 3)).reshape(nb, width, width)
    y = dot("takx,kxb->tab", xfull, ufull)
    yl = mask(y[:, :, None, :], None, cM)
    x = x - yl
    zp = dot("qtax,tacb->qxcb", urow, yl - xm)
    x = x + unpack_rows(scatter_rows(zp), rM) + mask(pivot_inverse, rM, cM)
    return x


def solution(mesh):
    in_specs = (P(None, "row", None, "col"), P(None, "row", None, "col"), P(), P())
    out_specs = P(None, "row", None, "col")
    return jax.shard_map(shards, mesh=mesh, in_specs=in_specs, out_specs=out_specs, check_vma=False)
```

time: 455 us -> 374 us (0.82)
  matrix products: 47.5 us -> 18.7 us
  waiting for transfers between devices: 338 us -> 313 us
  local copies, waits for them, and re-layouts: 38.6 us -> 17.2 us
  other arithmetic: 15.9 us -> 10.6 us
    dot_general x4, matrix products: 47.5 us -> 18.7 us  [dot(): jnp.einsum(spec, a, b, precision=HIGHEST, preferred_element_type=jnp.floa...]
    mul x8 -> x1, local copies, waits for them, and re-layouts: 26.7 us -> 0.14 us  [shards(): ufull * S.reshape(brows, n_row)[:, :, None, None]]
    all_gather x4 -> x6, waiting for transfers between devices: 263 us -> 246 us  [the longest x2 82 us: shards(): urow = lax.all_gather(uc, 'col')]
    mul x6 -> x4, other arithmetic: 13.7 us -> 5.09 us  [the longest x1 2.21 us: shards(): jnp.transpose(xg, (1, 2, 0, 3))[:, :, None]]
    reduce_scatter x2, waiting for transfers between devices: 73.5 us -> 65.3 us  [scatter_rows(): zr = lax.psum_scatter(zp, 'row', scatter_dimension=0, tiled=True)]
    all_gather x0 -> x2, local copies, waits for them, and re-layouts: none -> 5.88 us  [the longest x1 3.96 us: shards(): xg = lax.all_gather(xm, 'col')]
    reshape x7 -> x16, local copies, waits for them, and re-layouts: 9.73 us -> 4.97 us  [the longest x4 2.2 us: scatter_rows(): return zr.reshape(n_col // n_row, width, bcols, width)]
  transfers between devices with their start and end apart: 6 -> 8, of which waited for: 6 -> 8; matrix products, arithmetic and copies ran while one was open for 11% -> 7% of each run, Pallas kernels for 0% -> 0%
where the time goes in v1:
time: 374 us
  waiting for transfers between devices  313 us (84%)
  matrix products  18.7 us (5%)
  local copies, waits for them, and re-layouts  17.2 us (5%)
  between operations  13.7 us (4%)
  other arithmetic  10.6 us (3%)
    all_gather x2, waiting for transfers between devices, shards(): urow = lax.all_gather(uc, 'col')  82 us
    all_gather x1, waiting for transfers between devices, shards(): xg = lax.all_gather(xm, 'col')  71.6 us
    reduce_scatter x2, waiting for transfers between devices, scatter_rows(): zr = lax.psum_scatter(zp, 'row', scatter_dimension=0, tiled=True)  65.3 us
    all_gather x2, waiting for transfers between devices, shards(): ucol = lax.all_gather(uc, 'row')  46.8 us
    all_gather x1, waiting for transfers between devices, shards(): xg = lax.all_gather(xc, 'col')  45.2 us
    dot_general x4, matrix products, dot(): jnp.einsum(spec, a, b, precision=HIGHEST, preferred_element_type=jnp.floa...  18.7 us
  transfers between devices with their start and end apart: 8, of which 8 were waited for; matrix products, arithmetic and copies ran while one was open for 7% of the time, Pallas kernels for 0%

profile of v1, /device:TPU:0, one launch (start us, length us, event | category | flops | bytes accessed | tf_op | source)
XLA Modules:
  0.0 373.5 jit_solution(717872237624760248)
XLA Ops:
  6.5 0.7 compare_reduce_fusion
  7.2 0.7 compare_convert_fusion.2
  9.4 2.3 multiply_reduce_fusion.1
  11.6 0.7 reduce_sum.57
  12.4 0.7 reduce_sum.55
  13.1 0.7 all-gather.17.cloned.1.call-update
  13.9 24.2 %all-gather.15.cloned.1.call-done = f32[16,128,128]{2,1,0:T(8,128)} async-done(((f32[2,128,128]{2,1,0:T(8,128)}), f32[16,128,128]{2,1,0:T(8,128)}) %all-gather.15.cloned.1.call-update) | async-done | bytes 1048592 | tf_op jit(solution)/shard_map/all_gather | solution.py:65
  38.2 1.7 maximum_multiply_fusion
  40.1 45.2 %all-gather.13.cloned.1.call-done = f32[32,128,128]{2,1,0:T(8,128)} async-done(((f32[2,128,128]{2,1,0:T(8,128)}), f32[32,128,128]{2,1,0:T(8,128)}) %all-gather.13.cloned.1.call-update) | async-done | bytes 2097168 | tf_op jit(solution)/shard_map/all_gather | solution.py:64
  85.3 2.2 broadcast_multiply_fusion
  87.5 3.5 convolution_bitcast_fusion.2
  91.7 40.1 %all-gather.17.cloned.1.call-done = f32[32,128,128]{2,1,0:T(8,128)} async-done(((f32[2,128,128]{2,1,0:T(8,128)}), f32[32,128,128]{2,1,0:T(8,128)}) %all-gather.17.cloned.1.call-update) | async-done | bytes 2097168 | tf_op jit(solution)/shard_map/all_gather | solution.py:66
  131.8 1.9 copy.50
  133.7 1.9 convolution_bitcast_fusion
  135.6 1.5 copy.53
  137.2 0.5 all-gather.21.cloned.1.call-update
  138.3 32.0 %reduce-scatter.3.cloned.1.call-done = f32[256,256]{1,0:T(8,128)} async-done(((f32[2048,256]{1,0:T(8,128)}), f32[256,256]{1,0:T(8,128)}) %reduce-scatter.3.cloned.1.call-update) | async-done | bytes 262160 | tf_op jit(solution)/shard_map/reduce_scatter | solution.py:45
  170.3 1.1 reshape.167
  171.4 1.1 multiply_multiply_fusion
  172.6 0.7 all-gather.23.cloned.1.call-update
  173.5 22.5 %all-gather.21.cloned.1.call-done = f32[32,128,128]{2,1,0:T(8,128)} async-done(((f32[4,128,128]{2,1,0:T(8,128)}), f32[32,128,128]{2,1,0:T(8,128)}) %all-gather.21.cloned.1.call-update) | async-done | bytes 2097168 | tf_op jit(solution)/shard_map/all_gather | solution.py:82
  196.0 1.7 copy.59
  197.8 71.6 %all-gather.19.cloned.1.call-done = f32[64,128,2,128]{3,1,2,0:T(8,128)} async-done(((f32[4,128,2,128]{3,1,2,0:T(8,128)}), f32[64,128,2,128]{3,1,2,0:T(8,128)}) %all-gather.19.cloned.1.call-update) | async-done | bytes 8388624 | tf_op jit(solution)/shard_map/all_gather | solution.py:84
  269.4 4.0 %copy.57 = f32[16,4,128,2,128]{4,2,0,3,1:T(8,128)S(1)} copy(f32[16,4,128,2,128]{4,2,3,1,0:T(8,128)} %bitcast.81) | data formatting | bytes 16777216 | tf_op jit(solution)/shard_map/all_gather | solution.py:84
  273.4 7.4 %convolution_bitcast_fusion.1 = f32[4,128,128]{2,1,0:T(8,128)} fusion(f32[4,128,32,128]{3,1,2,0:T(8,128)S(1)} %bitcast.77, f32[32,128,128,1]{2,1,0,3:T(8,128)S(1)} %bitcast.85), kind=kOutput, calls=%fused_computation.3 | convolution fusion | flops 3221225472 | bytes 10747904 | tf_op jit(solution)/shard_map/takx,kxb->tab/dot_general | solution.py:11
  280.8 41.9 %all-gather.23.cloned.1.call-done = f32[64,128,128]{2,1,0:T(8,128)} async-done(((f32[4,128,128]{2,1,0:T(8,128)}), f32[64,128,128]{2,1,0:T(8,128)}) %all-gather.23.cloned.1.call-update) | async-done | bytes 4194320 | tf_op jit(solution)/shard_map/all_gather | solution.py:83
  322.7 5.9 %fusion.5 = f32[16,128,2,128,1]{1,3,2,4,0:T(8,128)S(1)} fusion(f32[16,4,128,128,1]{3,2,4,1,0:T(8,128)} %bitcast.86, f32[4,128,2,128]{3,1,2,0:T(8,128)S(1)} %copy-done.1, f32[4,128,128]{2,1,0:T(8,128)} %convolution_bitcast_fusion.1, f32[2]{0:T(128)S(1)} %get-tuple-element.16), kind=kOutput, calls=%fused_computation.14 | convolution fusion | flops 3221487616 | bytes 7077896 | tf_op jit(solution)/shard_map/qtax,tacb->qxcb/dot_general | solution.py:11
  328.6 1.9 copy.61
  330.8 33.3 %reduce-scatter.5.cloned.1.call-done = f32[256,256]{1,0:T(8,128)} async-done(((f32[2048,256]{1,0:T(8,128)}), f32[256,256]{1,0:T(8,128)}) %reduce-scatter.5.cloned.1.call-update) | async-done | bytes 262160 | tf_op jit(solution)/shard_map/reduce_scatter | solution.py:45
  364.0 1.1 reshape.176
  365.1 0.3 fusion.3
  365.5 1.2 copy.65
  (49 shorter events, 3.7 us)
Async XLA Ops:
  6.5 31.6 %all-gather.15.cloned.1.call-start = ((), (), s32[]{:S(2)}) async-start(), calls=%async_computation.5 | async-start | bytes 1179648 | tf_op jit(solution)/shard_map/all_gather | solution.py:65
  12.3 73.0 %all-gather.13.cloned.1.call-start = ((), (), s32[]{:S(2)}) async-start(), calls=%async_computation.4 | async-start | bytes 2228224 | tf_op jit(solution)/shard_map/all_gather | solution.py:64
  13.1 118.7 %all-gather.17.cloned.1.call-start = ((), (), s32[]{:S(2)}) async-start(), calls=%async_computation.6 | async-start | bytes 2228224 | tf_op jit(solution)/shard_map/all_gather | solution.py:66
  13.8 156.5 %reduce-scatter.3.cloned.1.call-start = ((), (), s32[]{:S(2)}) async-start(), calls=%async_computation.2 | async-start | bytes 2359296 | tf_op jit(solution)/shard_map/reduce_scatter | solution.py:45
  87.5 3.6 copy-start
  137.1 58.9 %all-gather.21.cloned.1.call-start = ((), (), s32[]{:S(2)}) async-start(), calls=%async_computation.8 | async-start | bytes 2359296 | tf_op jit(solution)/shard_map/all_gather | solution.py:82
  137.7 131.7 %all-gather.19.cloned.1.call-start = ((), (), s32[]{:S(2)}) async-start(), calls=%async_computation.7 | async-start | bytes 8912896 | tf_op jit(solution)/shard_map/all_gather | solution.py:84
  171.4 26.3 %copy-start.2 = (f32[2,128,2,128]{3,1,2,0:T(8,128)}, f32[2,128,2,128]{3,1,2,0:T(8,128)S(1)}, u32[]{:S(2)}) copy-start(f32[2,128,2,128]{3,1,2,0:T(8,128)S(1)} %copy.54) | copy-start | bytes 786436
  172.5 150.2 %all-gather.23.cloned.1.call-start = ((), (), s32[]{:S(2)}) async-start(), calls=%async_computation.9 | async-start | bytes 4456448 | tf_op jit(solution)/shard_map/all_gather | solution.py:83
  173.3 190.7 %reduce-scatter.5.cloned.1.call-start = ((), (), s32[]{:S(2)}) async-start(), calls=%async_computation.3 | async-start | bytes 2359296 | tf_op jit(solution)/shard_map/reduce_scatter | solution.py:45
  273.4 49.3 %copy-start.1 = (f32[4,128,2,128]{3,1,2,0:T(8,128)S(1)}, f32[4,128,2,128]{3,1,2,0:T(8,128)}, u32[]{:S(2)}) copy-start(f32[4,128,2,128]{3,1,2,0:T(8,128)} %multiply_multiply_fusion) | copy-start | bytes 1572868
  330.5 34.7 %copy-start.3 = (f32[2,128,2,128]{3,1,2,0:T(8,128)S(1)}, f32[2,128,2,128]{3,1,2,0:T(8,128)}, u32[]{:S(2)}) copy-start(f32[2,128,2,128]{3,1,2,0:T(8,128)} %copy-done.2) | copy-start | bytes 786436
  330.5 34.7 %copy-start.4 = (f32[4,128,128]{2,1,0:T(8,128)S(1)}, f32[4,128,128]{2,1,0:T(8,128)}, u32[]{:S(2)}) copy-start(f32[4,128,128]{2,1,0:T(8,128)} %convolution_bitcast_fusion.1) | copy-start | bytes 786436
Sparse Core Ops, SparseCore 0:
  12.4 25.6 all-gather.14
  40.3 44.9 all-gather.12
  87.4 44.2 all-gather.16
  137.3 33.0 reduce-scatter.2
  171.9 24.1 all-gather.20
  198.0 71.3 all-gather.18
  271.5 51.0 all-gather.22
  330.6 33.3 reduce-scatter.4

commit v2 on v1

--- a/solution.py
+++ b/solution.py
@@ -56,39 +56,39 @@
     rM2, cM2 = rows_of(member[last]), cols_of(member[last])
     x = mask(pivot_inverse, rM2, cM2)
 
-    S, M = struct[1], member[1]
-    rS, cS, rM, cM = rows_of(S), cols_of(S), rows_of(M), cols_of(M)
-    xm = mask(x, rS, cS)
-    xc = pack_rows(xm.sum(axis=2))
-    uc = pack_rows(mask(unit_factor, rS, cM).sum(axis=2))
-    xg = lax.all_gather(xc, "col")
-    ucol = lax.all_gather(uc, "row")
-    urow = lax.all_gather(uc, "col")
-    xfull = jnp.transpose(xg, (1, 2, 0, 3))[:, :, None] * S.reshape(bcols, n_col)[None, None, :, :, None]
+    S1, M1, S0, M0 = struct[1], member[1], struct[0], member[0]
+    rS1, cS1, rM1, cM1 = rows_of(S1), cols_of(S1), rows_of(M1), cols_of(M1)
+    rS0, cS0, rM0, cM0 = rows_of(S0), cols_of(S0), rows_of(M0), cols_of(M0)
+
+    xm = mask(x, rS1, cS1)
+    xc1 = pack_rows(xm.sum(axis=2))
+    uc1 = pack_rows(mask(unit_factor, rS1, cM1).sum(axis=2))
+    uc0 = mask(unit_factor, rS0, cM0).sum(axis=2)
+    gcol = lax.all_gather(jnp.concatenate([xc1, uc1, uc0], axis=0), "col")
+    grow = lax.all_gather(jnp.concatenate([uc1, uc0], axis=0), "row")
+    xg, urow1, urow0 = gcol[:, 0:2], gcol[:, 2:4], gcol[:, 4:8]
+    ucol1, ucol0 = grow[:, 0:2], grow[:, 2:6]
+
+    xfull = jnp.transpose(xg, (1, 2, 0, 3))[:, :, None] * S1.reshape(bcols, n_col)[None, None, :, :, None]
     xfull = xfull.reshape(2, width, nb, width)
-    ufull = jnp.concatenate([jnp.transpose(ucol, (1, 0, 2, 3))] * (brows // 2), axis=0)
-    ufull = (ufull * S.reshape(brows, n_row)[:, :, None, None]).reshape(nb, width, width)
+    ufull = jnp.concatenate([jnp.transpose(ucol1, (1, 0, 2, 3))] * (brows // 2), axis=0)
+    ufull = (ufull * S1.reshape(brows, n_row)[:, :, None, None]).reshape(nb, width, width)
     y = dot("pakx,kxb->pab", xfull, ufull)
-    yl = mask(unpack_rows(y, rS)[:, :, None, :], None, cM)
+    yl = mask(unpack_rows(y, rS1)[:, :, None, :], None, cM1)
     x = x - yl
     wc = pack_rows(yl - xm)
-    zp = dot("qpax,pacb->qxcb", urow, wc)
-    x = x + unpack_rows(scatter_rows(zp), rM) + mask(pivot_inverse, rM, cM)
+    zp = dot("qpax,pacb->qxcb", urow1, wc)
+    x = x + unpack_rows(scatter_rows(zp), rM1) + mask(pivot_inverse, rM1, cM1)
 
-    S, M = struct[0], member[0]
-    rS, cS, rM, cM = rows_of(S), cols_of(S), rows_of(M), cols_of(M)
-    xm = mask(x, rS, cS)
-    uc = mask(unit_factor, rS, cM).sum(axis=2)
-    ucol = lax.all_gather(uc, "row")
-    urow = lax.all_gather(uc, "col")
+    xm = mask(x, rS0, cS0)
     xg = lax.all_gather(xm, "col")
     xfull = jnp.transpose(xg, (1, 2, 3, 0, 4)).reshape(brows, width, nb, width)
-    ufull = jnp.transpose(ucol, (1, 0, 2, 3)).reshape(nb, width, width)
+    ufull = jnp.transpose(ucol0, (1, 0, 2, 3)).reshape(nb, width, width)
     y = dot("takx,kxb->tab", xfull, ufull)
-    yl = mask(y[:, :, None, :], None, cM)
+    yl = mask(y[:, :, None, :], None, cM0)
     x = x - yl
-    zp = dot("qtax,tacb->qxcb", urow, yl - xm)
-    x = x + unpack_rows(scatter_rows(zp), rM) + mask(pivot_inverse, rM, cM)
+    zp = dot("qtax,tacb->qxcb", urow0, yl - xm)
+    x = x + unpack_rows(scatter_rows(zp), rM0) + mask(pivot_inverse, rM0, cM0)
     return x
 
 

time: 374 us -> 298 us (0.80)
  waiting for transfers between devices: 313 us -> 235 us
  local copies, waits for them, and re-layouts: 17.2 us -> 21.9 us
    all_gather x5 -> x2, waiting for transfers between devices: 174 us -> 101 us  [the longest x1 71.4 us: shards(): gcol = lax.all_gather(jnp.concatenate([xc1, uc1, uc0], axis=0), 'col')]
    transpose x1 -> x4, local copies, waits for them, and re-layouts: 1.73 us -> 7.36 us  [the longest x1 4.11 us: shards(): jnp.transpose(xg, (1, 2, 0, 3))[:, :, None]]
    all_gather x1, waiting for transfers between devices: 71.6 us -> 67.7 us  [shards(): xg = lax.all_gather(xm, 'col')]
  transfers between devices with their start and end apart: 8 -> 5, of which waited for: 8 -> 5; matrix products, arithmetic and copies ran while one was open for 7% -> 2% of each run, Pallas kernels for 0% -> 0%
where the time goes in v2:
time: 298 us
  waiting for transfers between devices  235 us (79%)
  local copies, waits for them, and re-layouts  21.9 us (7%)
  matrix products  19.6 us (7%)
  between operations  13.4 us (4%)
  other arithmetic  7.81 us (3%)
    all_gather x1, waiting for transfers between devices, shards(): gcol = lax.all_gather(jnp.concatenate([xc1, uc1, uc0], axis=0), 'col')  71.4 us
    all_gather x1, waiting for transfers between devices, shards(): xg = lax.all_gather(xm, 'col')  67.7 us
    reduce_scatter x2, waiting for transfers between devices, scatter_rows(): zr = lax.psum_scatter(zp, 'row', scatter_dimension=0, tiled=True)  66.2 us
    all_gather x1, waiting for transfers between devices, shards(): grow = lax.all_gather(jnp.concatenate([uc1, uc0], axis=0), 'row')  29.2 us
    dot_general x4, matrix products, dot(): jnp.einsum(spec, a, b, precision=HIGHEST, preferred_element_type=jnp.floa...  19.6 us
  transfers between devices with their start and end apart: 5, of which 5 were waited for; matrix products, arithmetic and copies ran while one was open for 2% of the time, Pallas kernels for 0%

profile of v2, /device:TPU:0, one launch (start us, length us, event | category | flops | bytes accessed | tf_op | source)
XLA Modules:
  0.0 297.7 jit_solution(13382351770332743686)
XLA Ops:
  6.5 0.7 compare_reduce_fusion
  7.2 0.7 compare_convert_fusion.2
  8.7 0.2 fusion.18
  9.1 0.2 fusion.10
  9.4 1.6 multiply_reduce_fusion.1
  11.0 0.8 pad_maximum_fusion.1
  11.9 0.8 pad_maximum_fusion
  12.9 29.2 %all-gather.9.cloned.1.call-done = f32[48,128,128]{2,1,0:T(8,128)} async-done(((f32[6,128,128]{2,1,0:T(8,128)}), f32[48,128,128]{2,1,0:T(8,128)}) %all-gather.9.cloned.1.call-update) | async-done | bytes 3145744 | tf_op jit(solution)/shard_map/all_gather | solution.py:68
  42.1 1.3 slice_bitcast_fusion.4
  43.8 71.4 %all-gather.7.cloned.1.call-done = f32[128,128,128]{2,1,0:T(8,128)} async-done(((f32[8,128,128]{2,1,0:T(8,128)}), f32[128,128,128]{2,1,0:T(8,128)}) %all-gather.7.cloned.1.call-update) | async-done | bytes 8388624 | tf_op jit(solution)/shard_map/all_gather | solution.py:67
  115.2 4.1 %slice_bitcast_fusion.3 = (f32[2,128,16,128]{3,1,0,2:T(8,128)S(1)}, f32[16,2,128,128]{3,2,1,0:T(8,128)}) fusion(f32[16,8,128,128]{3,2,1,0:T(8,128)} %bitcast.79), kind=kLoop, calls=%fused_computation.3 | loop fusion | bytes 8388608 | tf_op jit(solution)/shard_map/transpose | solution.py:72
  119.3 0.6 broadcast_multiply_fusion
  119.9 3.5 %convolution_bitcast_fusion.2 = f32[2,128,128]{2,1,0:T(8,128)S(1)} fusion(f32[2,128,32,128]{3,1,2,0:T(8,128)S(1)} %bitcast.76, f32[32,128,128,1]{2,1,0,3:T(8,128)S(1)} %bitcast.77), kind=kOutput, calls=%fused_computation.8 | convolution fusion | flops 1610612736 | bytes 6422528 | tf_op jit(solution)/shard_map/pakx,kxb->pab/dot_general | solution.py:11
  123.6 0.7 reduce_sum.59
  124.4 1.2 copy.95
  125.7 3.5 %convolution_bitcast_fusion = f32[8,2,128,256]{3,2,0,1:T(8,128)S(1)} fusion(f32[2,8,128,128,2]{2,3,4,1,0:T(8,128)S(1)} %bitcast.84, f32[256,128,2,1,1]{1,0,2,4,3:T(8,128)S(1)} %bitcast.89), kind=kOutput, calls=%fused_computation.6 | convolution fusion | flops 1610612736 | bytes 4456448 | tf_op jit(solution)/shard_map/qpax,pacb->qxcb/dot_general | solution.py:11
  129.2 1.5 copy.56
  131.4 32.9 %reduce-scatter.3.cloned.1.call-done = f32[256,256]{1,0:T(8,128)} async-done(((f32[2048,256]{1,0:T(8,128)}), f32[256,256]{1,0:T(8,128)}) %reduce-scatter.3.cloned.1.call-update) | async-done | bytes 262160 | tf_op jit(solution)/shard_map/reduce_scatter | solution.py:45
  164.3 1.1 reshape.169
  165.4 1.1 multiply_multiply_fusion
  166.5 0.2 reduce-scatter.5.cloned.1.call-start
  166.7 1.7 slice_bitcast_fusion.2
  168.5 0.2 copy.61
  168.7 67.7 %all-gather.11.cloned.1.call-done = f32[64,128,2,128]{3,1,2,0:T(8,128)} async-done(((f32[4,128,2,128]{3,1,2,0:T(8,128)}), f32[64,128,2,128]{3,1,2,0:T(8,128)}) %all-gather.11.cloned.1.call-update) | async-done | bytes 8388624 | tf_op jit(solution)/shard_map/all_gather | solution.py:84
  236.4 4.0 %copy.60 = f32[16,4,128,2,128]{4,2,0,3,1:T(8,128)S(1)} copy(f32[16,4,128,2,128]{4,2,3,1,0:T(8,128)} %bitcast.81) | data formatting | bytes 16777216 | tf_op jit(solution)/shard_map/all_gather | solution.py:84
  240.4 6.7 %convolution_bitcast_fusion.1 = f32[4,128,128]{2,1,0:T(8,128)S(1)} fusion(f32[4,128,32,128]{3,1,2,0:T(8,128)S(1)} %bitcast.75, f32[32,128,128,1]{2,1,0,3:T(8,128)S(1)} %bitcast.85), kind=kOutput, calls=%fused_computation.7 | convolution fusion | flops 3221225472 | bytes 10747904 | tf_op jit(solution)/shard_map/takx,kxb->tab/dot_general | solution.py:11
  247.1 5.9 %fusion = f32[16,128,2,128,1]{1,3,2,4,0:T(8,128)S(1)} fusion(f32[16,8,128,128]{3,2,1,0:T(8,128)} %bitcast.80, f32[4,128,2,128]{3,1,2,0:T(8,128)S(1)} %copy-done.2, f32[4,128,128]{2,1,0:T(8,128)S(1)} %convolution_bitcast_fusion.1, f32[2]{0:T(128)S(1)} %get-tuple-element.18), kind=kOutput, calls=%fused_computation.1 | convolution fusion | flops 3221487616 | bytes 7077896 | tf_op jit(solution)/shard_map/qtax,tacb->qxcb/dot_general | solution.py:11
  253.1 1.9 copy.63
  255.2 33.3 %reduce-scatter.5.cloned.1.call-done = f32[256,256]{1,0:T(8,128)} async-done(((f32[2048,256]{1,0:T(8,128)}), f32[256,256]{1,0:T(8,128)}) %reduce-scatter.5.cloned.1.call-update) | async-done | bytes 262160 | tf_op jit(solution)/shard_map/reduce_scatter | solution.py:45
  288.5 1.1 reshape.176
  289.6 0.3 fusion.4
  289.9 1.2 copy.67
  (40 shorter events, 2.9 us)
Async XLA Ops:
  6.5 35.6 %all-gather.9.cloned.1.call-start = ((), (), s32[]{:S(2)}) async-start(), calls=%async_computation.5 | async-start | bytes 3538944 | tf_op jit(solution)/shard_map/all_gather | solution.py:68
  11.8 103.4 %all-gather.7.cloned.1.call-start = ((), (), s32[]{:S(2)}) async-start(), calls=%async_computation.4 | async-start | bytes 8912896 | tf_op jit(solution)/shard_map/all_gather | solution.py:67
  12.7 151.6 %reduce-scatter.3.cloned.1.call-start = ((), (), s32[]{:S(2)}) async-start(), calls=%async_computation.2 | async-start | bytes 2359296 | tf_op jit(solution)/shard_map/reduce_scatter | solution.py:45
  119.8 3.6 %copy-start = (f32[4,128,2,128]{3,2,1,0:T(2,128)S(1)}, f32[4,128,2,128]{3,2,1,0:T(2,128)}, u32[]{:S(2)}) copy-start(f32[4,128,2,128]{3,2,1,0:T(2,128)} %param.5) | copy-start | bytes 1572868
  123.3 2.3 copy-start.1
  130.8 105.6 %all-gather.11.cloned.1.call-start = ((), (), s32[]{:S(2)}) async-start(), calls=%async_computation.6 | async-start | bytes 8912896 | tf_op jit(solution)/shard_map/all_gather | solution.py:84
  166.5 122.0 %reduce-scatter.5.cloned.1.call-start = ((), (), s32[]{:S(2)}) async-start(), calls=%async_computation.3 | async-start | bytes 2359296 | tf_op jit(solution)/shard_map/reduce_scatter | solution.py:45
  240.4 6.7 %copy-start.2 = (f32[4,128,2,128]{3,1,2,0:T(8,128)S(1)}, f32[4,128,2,128]{3,1,2,0:T(8,128)}, u32[]{:S(2)}) copy-start(f32[4,128,2,128]{3,1,2,0:T(8,128)} %multiply_multiply_fusion) | copy-start | bytes 1572868
Sparse Core Ops, SparseCore 0:
  11.9 30.1 all-gather.8
  44.2 70.8 all-gather.6
  130.9 33.3 reduce-scatter.2
  166.6 69.7 all-gather.10
  255.1 33.3 reduce-scatter.4

commit v3 on v2

--- a/solution.py
+++ b/solution.py
@@ -3,12 +3,35 @@
 from jax import lax
 from jax.sharding import PartitionSpec as P
 
+
 SUPERNODES = 3
 HIGHEST = lax.Precision.HIGHEST
+ROW_STAGES = ((1, 2), (2, 4))
+COL_STAGES = ((1, 4), (4, 4))
 
 
 def dot(spec, a, b):
     return jnp.einsum(spec, a, b, precision=HIGHEST, preferred_element_type=jnp.float32)
+
+
+def pp_gather(a, axis, stages):
+    n = lax.axis_size(axis)
+    me = lax.axis_index(axis)
+    out = a[None]
+    for stride, count in stages:
+        def to(i, d, stride=stride, count=count):
+            digit = (i // stride) % count
+            return i + (((digit + d) % count) - digit) * stride
+
+        parts = [out] + [lax.ppermute(out, axis, [(i, to(i, d)) for i in range(n)]) for d in range(1, count)]
+        out = jnp.concatenate(parts, axis=0)
+    src = jnp.arange(n)
+    at = jnp.zeros((n,), jnp.int32)
+    mult = 1
+    for stride, count in stages:
+        at = at + ((me // stride - src // stride) % count) * mult
+        mult *= count
+    return jnp.take(out, at, axis=0)
 
 
 def shards(unit_factor, pivot_inverse, supernode, row_bits):
@@ -65,7 +88,7 @@
     uc1 = pack_rows(mask(unit_factor, rS1, cM1).sum(axis=2))
     uc0 = mask(unit_factor, rS0, cM0).sum(axis=2)
     gcol = lax.all_gather(jnp.concatenate([xc1, uc1, uc0], axis=0), "col")
-    grow = lax.all_gather(jnp.concatenate([uc1, uc0], axis=0), "row")
+    grow = pp_gather(jnp.concatenate([uc1, uc0], axis=0), "row", ROW_STAGES)
     xg, urow1, urow0 = gcol[:, 0:2], gcol[:, 2:4], gcol[:, 4:8]
     ucol1, ucol0 = grow[:, 0:2], grow[:, 2:6]
 
@@ -78,13 +101,20 @@
     x = x - yl
     wc = pack_rows(yl - xm)
     zp = dot("qpax,pacb->qxcb", urow1, wc)
-    x = x + unpack_rows(scatter_rows(zp), rM1) + mask(pivot_inverse, rM1, cM1)
 
     xm = mask(x, rS0, cS0)
-    xg = lax.all_gather(xm, "col")
+    early, zp = lax.optimization_barrier((pack_rows(mask(xm, rM2)), zp))
+    g_early = pp_gather(early, "col", COL_STAGES)
+    z1 = scatter_rows(zp)
+    x = x + unpack_rows(z1, rM1) + mask(pivot_inverse, rM1, cM1)
+    xm = mask(x, rS0, cS0)
+    late = pack_rows(mask(xm, rM1))
+    g_late = lax.all_gather(late, "col")
+    xg = jnp.concatenate([g_early, g_late], axis=1)
     xfull = jnp.transpose(xg, (1, 2, 3, 0, 4)).reshape(brows, width, nb, width)
     ufull = jnp.transpose(ucol0, (1, 0, 2, 3)).reshape(nb, width, width)
     y = dot("takx,kxb->tab", xfull, ufull)
+    y = unpack_rows(y[0:2], rM2) + unpack_rows(y[2:4], rM1)
     yl = mask(y[:, :, None, :], None, cM0)
     x = x - yl
     zp = dot("qtax,tacb->qxcb", urow0, yl - xm)

time: 298 us -> 334 us (1.12)
  waiting for transfers between devices: 235 us -> 188 us
  local copies, waits for them, and re-layouts: 21.9 us -> 56.6 us
  other arithmetic: 7.81 us -> 35.2 us
  starting transfers between devices: 0.35 us -> 16 us
  matrix products: 19.6 us -> 23.1 us
    ppermute x0 -> x10, waiting for transfers between devices: none -> 97.4 us  [pp_gather(): lax.ppermute(out, axis, [(i, to(i, d)) for i in range(n)])]
    all_gather x2 -> x1, waiting for transfers between devices: 97 us -> 0.01 us  [shards(): g_late = lax.all_gather(late, 'col')]
    all_gather x1, waiting for transfers between devices: 71.4 us -> 22.6 us  [shards(): gcol = lax.all_gather(jnp.concatenate([xc1, uc1, uc0], axis=0), 'col')]
    ppermute x0 -> x10, starting transfers between devices: none -> 15.9 us  [pp_gather(): lax.ppermute(out, axis, [(i, to(i, d)) for i in range(n)])]
    unnamed x7 -> x53, local copies, waits for them, and re-layouts: 1.17 us -> 10.5 us
    gather x0 -> x2, local copies, waits for them, and re-layouts: none -> 7.46 us  [pp_gather(): return jnp.take(out, at, axis=0)]
    select_n x0 -> x4, other arithmetic: none -> 7.11 us  [pp_gather(): return jnp.take(out, at, axis=0)]
    all_gather x1, local copies, waits for them, and re-layouts: 3.96 us -> 9 us  [shards(): gcol = lax.all_gather(jnp.concatenate([xc1, uc1, uc0], axis=0), 'col')]
  transfers between devices with their start and end apart: 5 -> 14, of which waited for: 5 -> 11; matrix products, arithmetic and copies ran while one was open for 2% -> 11% of each run, Pallas kernels for 0% -> 0%
where the time goes in v3:
time: 334 us; the launch traced here: 332 us
  waiting for transfers between devices  188 us (56%)
  local copies, waits for them, and re-layouts  56.6 us (17%)
  other arithmetic  35.2 us (11%)
  matrix products  23.1 us (7%)
  starting transfers between devices  16 us (5%)
  between operations  13.6 us (4%)
    ppermute x10, waiting for transfers between devices, pp_gather(): lax.ppermute(out, axis, [(i, to(i, d)) for i in range(n)])  97.4 us
    reduce_scatter x2, waiting for transfers between devices, scatter_rows(): zr = lax.psum_scatter(zp, 'row', scatter_dimension=0, tiled=True)  67.9 us
    dot_general x4, matrix products, dot(): jnp.einsum(spec, a, b, precision=HIGHEST, preferred_element_type=jnp.floa...  23.1 us
    all_gather x1, waiting for transfers between devices, shards(): gcol = lax.all_gather(jnp.concatenate([xc1, uc1, uc0], axis=0), 'col')  22.6 us
    ppermute x10, starting transfers between devices, pp_gather(): lax.ppermute(out, axis, [(i, to(i, d)) for i in range(n)])  15.9 us
    unnamed x53, local copies, waits for them, and re-layouts  10.5 us
    all_gather x1, local copies, waits for them, and re-layouts, shards(): gcol = lax.all_gather(jnp.concatenate([xc1, uc1, uc0], axis=0), 'col')  9 us
    gather x2, local copies, waits for them, and re-layouts, pp_gather(): return jnp.take(out, at, axis=0)  7.46 us
  transfers between devices with their start and end apart: 14, of which 11 were waited for; matrix products, arithmetic and copies ran while one was open for 11% of the time, Pallas kernels for 0%

profile of v3, /device:TPU:0, one launch (start us, length us, event | category | flops | bytes accessed | tf_op | source)
XLA Modules:
  0.0 332.5 jit_solution(3411036198850430416)
XLA Ops:
  9.5 3.5 %fusion.46 = (f32[4,128,128]{2,1,0:T(8,128)S(1)}, f32[4,128,2,128]{3,2,1,0:T(2,128)}, f32[4,128,128]{2,1,0:T(8,128)S(1)}, f32[4,128,128]{2,1,0:T(8,128)S(1)}) fusion(f32[2]{0:T(128)S(1)} %get-tuple-element.29, f32[4]{0:T(128)S(1)} %get-tuple-element.27, f32[2]{0:T(128)S(1)} %get-tuple-element.28, f32[4,128,2,128]{3,2,1,0:T(2,128)} %param.5, ...), kind=kLoop, calls=%fused_computation.155 | loop fusion | flops 1245184 | bytes 2359376 | tf_op jit(solution)/shard_map/reduce_sum | solution.py:87
  18.4 2.7 collective-permute-start.2
  25.1 12.8 %collective-permute-done.1 = f32[2,6,128,128]{3,2,1,0:T(8,128)} collective-permute-done((f32[2,6,128,128]{3,2,1,0:T(8,128)}, f32[2,6,128,128]{3,2,1,0:T(8,128)}, u32[]{:S(2)}, u32[]{:S(2)}) %collective-permute-start.1) | collective-permute-done | bytes 786464 | tf_op jit(solution)/shard_map/ppermute | solution.py:26
  39.1 16.7 %collective-permute-done.2 = f32[2,6,128,128]{3,2,1,0:T(8,128)} collective-permute-done((f32[2,6,128,128]{3,2,1,0:T(8,128)}, f32[2,6,128,128]{3,2,1,0:T(8,128)}, u32[]{:S(2)}, u32[]{:S(2)}) %collective-permute-start.2) | collective-permute-done | bytes 786464 | tf_op jit(solution)/shard_map/ppermute | solution.py:26
  58.3 2.5 gather_fusion
  60.9 2.2 broadcast_select_fusion.1
  64.9 22.6 %all-gather.5.cloned.1.call-done = f32[128,128,128]{2,1,0:T(8,128)} async-done(((f32[8,128,128]{2,1,0:T(8,128)}), f32[128,128,128]{2,1,0:T(8,128)}) %all-gather.5.cloned.1.call-update) | async-done | bytes 8388624 | tf_op jit(solution)/shard_map/all_gather | solution.py:90
  87.5 9.0 %copy.57 = f32[128,128,128]{1,2,0:T(8,128)} copy(f32[128,128,128]{2,1,0:T(8,128)} %all-gather.5.cloned.1.call-done) | data formatting | bytes 16777216 | tf_op jit(solution)/shard_map/all_gather | solution.py:90
  96.5 3.1 slice_bitcast_fusion.5
  99.7 3.0 copy.58
  102.6 2.3 broadcast_multiply_fusion
  105.0 3.5 %convolution_bitcast_fusion.1 = f32[2,128,128]{2,1,0:T(8,128)S(1)} fusion(f32[2,128,32,128]{3,1,2,0:T(8,128)S(1)} %bitcast.86, f32[32,128,128,1]{2,1,0,3:T(8,128)S(1)} %bitcast.87), kind=kOutput, calls=%fused_computation.15 | convolution fusion | flops 1610612736 | bytes 6422528 | tf_op jit(solution)/shard_map/pakx,kxb->pab/dot_general | solution.py:14
  110.3 2.1 reduce_sum.78
  112.4 2.1 reduce_sum.77
  114.5 4.8 %fusion.2 = f32[16,128,2,128]{3,1,2,0:T(8,128)} fusion(f32[16,8,128,128]{2,3,1,0:T(8,128)} %bitcast.83, f32[2,128,2,128]{3,2,1,0:T(2,128)} %reduce_sum.78), kind=kOutput, calls=%fused_computation.12 | convolution fusion | flops 1610612736 | bytes 4456448 | tf_op jit(solution)/shard_map/qpax,pacb->qxcb/dot_general | solution.py:14
  119.3 2.9 copy.62
  122.2 3.0 copy.63
  125.5 33.3 %reduce-scatter.3.cloned.1.call-done = f32[256,256]{1,0:T(8,128)} async-done(((f32[2048,256]{1,0:T(8,128)}), f32[256,256]{1,0:T(8,128)}) %reduce-scatter.3.cloned.1.call-update) | async-done | bytes 262160 | tf_op jit(solution)/shard_map/reduce_scatter | solution.py:68
  160.6 3.1 fusion.8
  167.6 2.7 collective-permute-start.6
  172.0 8.5 %collective-permute-done.6 = f32[1,2,128,2,128]{4,2,3,1,0:T(8,128)S(1)} collective-permute-done((f32[1,2,128,2,128]{4,2,3,1,0:T(8,128)}, f32[1,2,128,2,128]{4,2,3,1,0:T(8,128)S(1)}, u32[]{:S(2)}, u32[]{:S(2)}) %collective-permute-start.6) | collective-permute-done | bytes 262176 | tf_op jit(solution)/shard_map/ppermute | solution.py:26
  181.4 4.3 %collective-permute-done.4 = f32[1,2,128,2,128]{4,2,3,1,0:T(8,128)} collective-permute-done((f32[1,2,128,2,128]{4,2,3,1,0:T(8,128)}, f32[1,2,128,2,128]{4,2,3,1,0:T(8,128)}, u32[]{:S(2)}, u32[]{:S(2)}) %collective-permute-start.4) | collective-permute-done | bytes 262176 | tf_op jit(solution)/shard_map/ppermute | solution.py:26
  190.4 2.3 collective-permute-start.8
  197.9 29.3 %collective-permute-done.7 = f32[4,2,128,2,128]{4,2,3,1,0:T(8,128)S(1)} collective-permute-done((f32[4,2,128,2,128]{4,2,3,1,0:T(8,128)S(1)}, f32[4,2,128,2,128]{4,2,3,1,0:T(8,128)S(1)}, u32[]{:S(2)}, u32[]{:S(2)}) %collective-permute-start.7) | collective-permute-done | bytes 1048608 | tf_op jit(solution)/shard_map/ppermute | solution.py:26
  228.3 23.0 %collective-permute-done.8 = f32[4,2,128,2,128]{4,2,3,1,0:T(8,128)S(1)} collective-permute-done((f32[4,2,128,2,128]{4,2,3,1,0:T(8,128)S(1)}, f32[4,2,128,2,128]{4,2,3,1,0:T(8,128)S(1)}, u32[]{:S(2)}, u32[]{:S(2)}) %collective-permute-start.8) | collective-permute-done | bytes 1048608 | tf_op jit(solution)/shard_map/ppermute | solution.py:26
  253.4 4.9 %gather_fusion.1 = f32[16,2,128,2,128]{4,2,3,1,0:T(8,128)} fusion(f32[16,2,128,2,128]{4,2,3,1,0:T(8,128)} %constant_dynamic-update-slice_fusion.5, s32[1024]{0:T(1024)S(1)} %pad_clamp_fusion), kind=kCustom, calls=%fused_computation.1 | custom fusion | bytes 8388672 | tf_op jit(solution)/shard_map/jit(_take)/gather | solution.py:34
  258.3 4.8 %broadcast_select_fusion = f32[16,2,128,2,128]{4,2,3,1,0:T(8,128)} fusion(f32[16,2,128,2,128]{4,2,3,1,0:T(8,128)} %gather_fusion.1, pred[16]{0:T(512)(128)(4,1)S(1)} %compare_and_fusion), kind=kLoop, calls=%fused_computation.10 | loop fusion | flops 1048576 | bytes 8388624 | tf_op jit(solution)/shard_map/jit(_take)/select_n | solution.py:34
  263.2 4.0 %maximum_bitcast_fusion = f32[4,128,2,16,128]{4,1,2,0,3:T(8,128)S(1)} fusion(f32[16,2,128,2,128]{4,2,3,1,0:T(8,128)} %bitcast.93, f32[16,2,128,2,128]{4,2,3,1,0:T(8,128)} %broadcast_select_fusion), kind=kLoop, calls=%fused_computation.2 | loop fusion | flops 2097152 | bytes 16777216 | tf_op jit(solution)/shard_map/transpose | solution.py:114
  267.2 3.8 %copy.66 = f32[4,128,2,16,128]{4,1,3,2,0:T(8,128)} copy(f32[4,128,2,16,128]{4,1,2,0,3:T(8,128)S(1)} %maximum_bitcast_fusion) | data formatting | bytes 16777216 | tf_op jit(solution)/shard_map/transpose | solution.py:114
  271.0 9.2 %convolution_bitcast_fusion = f32[4,128,128]{2,1,0:T(8,128)S(1)} fusion(f32[4,128,32,128]{3,1,2,0:T(8,128)} %bitcast.85, f32[32,128,128,1]{2,1,0,3:T(8,128)S(1)} %bitcast.92), kind=kOutput, calls=%fused_computation.14 | convolution fusion | flops 3221225472 | bytes 10747904 | tf_op jit(solution)/shard_map/takx,kxb->tab/dot_general | solution.py:14
  280.9 5.7 %fusion = f32[16,128,2,128,1]{1,3,4,2,0:T(8,128)S(1)} fusion(f32[16,8,128,128]{2,3,1,0:T(8,128)} %bitcast.84, f32[4,128,2,128]{1,3,0,2:T(8,128)S(1)} %copy.69), kind=kOutput, calls=%fused_computation.4 | convolution fusion | flops 3221225472 | bytes 6815744 | tf_op jit(solution)/shard_map/qtax,tacb->qxcb/dot_general | solution.py:14
  288.8 34.7 %reduce-scatter.5.cloned.1.call-done = f32[256,256]{1,0:T(8,128)} async-done(((f32[2048,256]{1,0:T(8,128)}), f32[256,256]{1,0:T(8,128)}) %reduce-scatter.5.cloned.1.call-update) | async-done | bytes 262160 | tf_op jit(solution)/shard_map/reduce_scatter | solution.py:68
  (126 shorter events, 46.3 us)
Async XLA Ops:
  6.5 81.0 %all-gather.5.cloned.1.call-start = ((), (), s32[]{:S(2)}) async-start(), calls=%async_computation.4 | async-start | bytes 8912896 | tf_op jit(solution)/shard_map/all_gather | solution.py:90
  7.9 5.1 %copy-start.19 = (f32[32]{0:T(128)}, f32[32]{0:T(128)S(1)}, u32[]{:S(2)}) copy-start(f32[32]{0:T(128)S(1)} %get-tuple-element.22) | copy-start | bytes 388
  8.8 4.2 %copy-start.7 = (f32[2]{0:T(128)}, f32[2]{0:T(128)S(1)}, u32[]{:S(2)}) copy-start(f32[2]{0:T(128)S(1)} %get-tuple-element.30) | copy-start | bytes 28
  8.8 4.2 %copy-start.11 = (f32[2]{0:T(128)}, f32[2]{0:T(128)S(1)}, u32[]{:S(2)}) copy-start(f32[2]{0:T(128)S(1)} %get-tuple-element.31) | copy-start | bytes 28
  9.1 4.0 %copy-start.9 = (f32[2]{0:T(128)}, f32[2]{0:T(128)S(1)}, u32[]{:S(2)}) copy-start(f32[2]{0:T(128)S(1)} %get-tuple-element.28) | copy-start | bytes 28
  9.5 3.6 %copy-start.13 = (f32[4]{0:T(128)}, f32[4]{0:T(128)S(1)}, u32[]{:S(2)}) copy-start(f32[4]{0:T(128)S(1)} %get-tuple-element.27) | copy-start | bytes 52
  13.9 144.9 %reduce-scatter.3.cloned.1.call-start = ((), (), s32[]{:S(2)}) async-start(), calls=%async_computation.2 | async-start | bytes 2359296 | tf_op jit(solution)/shard_map/reduce_scatter | solution.py:68
  14.0 1.8 collective-permute-start
  15.8 7.7 %copy-start.6 = (f32[1,6,128,128]{3,2,1,0:T(8,128)}, f32[1,6,128,128]{3,2,1,0:T(8,128)S(1)}, u32[]{:S(2)}) copy-start(f32[1,6,128,128]{3,2,1,0:T(8,128)S(1)} %collective-permute-done) | copy-start | bytes 1179652
  16.8 21.1 %collective-permute-start.1 = (f32[2,6,128,128]{3,2,1,0:T(8,128)}, f32[2,6,128,128]{3,2,1,0:T(8,128)}, u32[]{:S(2)}, u32[]{:S(2)}) collective-permute-start(f32[2,6,128,128]{3,2,1,0:T(8,128)} %pad_maximum_fusion.1), channel_id=1, source_target_pairs={{0,32},{16,48},{32,64},{48,80},{64,96},{80,112},{96,0},{112,16},{1... | collective-permute-start | bytes 2359304 | tf_op jit(solution)/shard_map/ppermute | solution.py:26
  18.4 37.5 %collective-permute-start.2 = (f32[2,6,128,128]{3,2,1,0:T(8,128)}, f32[2,6,128,128]{3,2,1,0:T(8,128)}, u32[]{:S(2)}, u32[]{:S(2)}) collective-permute-start(f32[2,6,128,128]{3,2,1,0:T(8,128)} %pad_maximum_fusion.1), channel_id=1, source_target_pairs={{0,64},{16,80},{32,96},{48,112},{64,0},{80,16},{96,32},{112,48},{1... | collective-permute-start | bytes 2359304 | tf_op jit(solution)/shard_map/ppermute | solution.py:26
  21.2 35.9 %collective-permute-start.3 = (f32[2,6,128,128]{3,2,1,0:T(8,128)}, f32[2,6,128,128]{3,2,1,0:T(8,128)}, u32[]{:S(2)}, u32[]{:S(2)}) collective-permute-start(f32[2,6,128,128]{3,2,1,0:T(8,128)} %pad_maximum_fusion.1), channel_id=1, source_target_pairs={{0,96},{16,112},{32,0},{48,16},{64,32},{80,48},{96,64},{112,80},{1... | collective-permute-start | bytes 2359304 | tf_op jit(solution)/shard_map/ppermute | solution.py:26
  57.1 3.8 %copy-start.21 = (pred[8]{0:T(512)(128)(4,1)S(1)}, pred[8]{0:T(512)(128)(4,1)}, u32[]{:S(2)}) copy-start(pred[8]{0:T(512)(128)(4,1)} %compare_and_fusion.1) | copy-start | bytes 28
  96.5 6.1 %copy-start.16 = (f32[2,16]{1,0:T(2,128)S(1)}, f32[2,16]{1,0:T(2,128)}, u32[]{:S(2)}) copy-start(f32[2,16]{1,0:T(2,128)} %copy-done.15) | copy-start | bytes 388
  105.0 3.5 %copy-start.14 = (f32[4]{0:T(128)S(1)}, f32[4]{0:T(128)}, u32[]{:S(2)}) copy-start(f32[4]{0:T(128)} %copy-done.13) | copy-start | bytes 52
  105.0 3.6 %copy-start.1 = (f32[4,128,2,128]{3,2,1,0:T(2,128)S(1)}, f32[4,128,2,128]{3,2,1,0:T(2,128)}, u32[]{:S(2)}) copy-start(f32[4,128,2,128]{3,2,1,0:T(2,128)} %param.5) | copy-start | bytes 1572868
  105.0 3.6 %copy-start.5 = (f32[4,128,2,128]{3,2,1,0:T(2,128)S(1)}, f32[4,128,2,128]{3,2,1,0:T(2,128)}, u32[]{:S(2)}) copy-start(f32[4,128,2,128]{3,2,1,0:T(2,128)} %get-tuple-element.14) | copy-start | bytes 1572868
  105.0 3.6 %copy-start.8 = (f32[2]{0:T(128)S(1)}, f32[2]{0:T(128)}, u32[]{:S(2)}) copy-start(f32[2]{0:T(128)} %copy-done.7) | copy-start | bytes 28
  105.0 3.6 %copy-start.10 = (f32[2]{0:T(128)S(1)}, f32[2]{0:T(128)}, u32[]{:S(2)}) copy-start(f32[2]{0:T(128)} %copy-done.9) | copy-start | bytes 28
  122.2 3.0 copy-start.20
  125.2 138.0 %all-gather.7.cloned.1.call-start = ((), (), s32[]{:S(2)}) async-start(), calls=%async_computation.5 | async-start | bytes 4456448 | tf_op jit(solution)/shard_map/all_gather | solution.py:112
  165.9 157.6 %reduce-scatter.5.cloned.1.call-start = ((), (), s32[]{:S(2)}) async-start(), calls=%async_computation.3 | async-start | bytes 2359296 | tf_op jit(solution)/shard_map/reduce_scatter | solution.py:68
  167.6 12.9 %collective-permute-start.6 = (f32[1,2,128,2,128]{4,2,3,1,0:T(8,128)}, f32[1,2,128,2,128]{4,2,3,1,0:T(8,128)S(1)}, u32[]{:S(2)}, u32[]{:S(2)}) collective-permute-start(f32[1,2,128,2,128]{4,2,3,1,0:T(8,128)} %bitcast.81), channel_id=1, source_target_pairs={{0,3},{1,0},{2,1},{3,2},{4,7},{5,4},{6,5},{7,6},{8,11},{9,8},{10,9... | collective-permute-start | bytes 786440 | tf_op jit(solution)/shard_map/ppermute | solution.py:26
  170.3 11.2 %collective-permute-start.5 = (f32[1,2,128,2,128]{4,2,3,1,0:T(8,128)}, f32[1,2,128,2,128]{4,2,3,1,0:T(8,128)}, u32[]{:S(2)}, u32[]{:S(2)}) collective-permute-start(f32[1,2,128,2,128]{4,2,3,1,0:T(8,128)} %bitcast.81), channel_id=1, source_target_pairs={{0,2},{1,3},{2,0},{3,1},{4,6},{5,7},{6,4},{7,5},{8,10},{9,11},{10,... | collective-permute-start | bytes 786440 | tf_op jit(solution)/shard_map/ppermute | solution.py:26
  171.1 14.7 %collective-permute-start.4 = (f32[1,2,128,2,128]{4,2,3,1,0:T(8,128)}, f32[1,2,128,2,128]{4,2,3,1,0:T(8,128)}, u32[]{:S(2)}, u32[]{:S(2)}) collective-permute-start(f32[1,2,128,2,128]{4,2,3,1,0:T(8,128)} %bitcast.81), channel_id=1, source_target_pairs={{0,1},{1,2},{2,3},{3,0},{4,5},{5,6},{6,7},{7,4},{8,9},{9,10},{10,1... | collective-permute-start | bytes 786440 | tf_op jit(solution)/shard_map/ppermute | solution.py:26
  186.9 40.3 %collective-permute-start.7 = (f32[4,2,128,2,128]{4,2,3,1,0:T(8,128)S(1)}, f32[4,2,128,2,128]{4,2,3,1,0:T(8,128)S(1)}, u32[]{:S(2)}, u32[]{:S(2)}) collective-permute-start(f32[4,2,128,2,128]{4,2,3,1,0:T(8,128)S(1)} %pad_maximum_fusion), channel_id=1, source_target_pairs={{0,4},{1,5},{2,6},{3,7},{4,8},{5,9},{6,10},{7,11},{8,12},{9,13},{1... | collective-permute-start | bytes 3145736 | tf_op jit(solution)/shard_map/ppermute | solution.py:26
  189.0 4.1 %copy-start.4 = (f32[2,128,2,128]{3,2,1,0:T(2,128)S(1)}, f32[2,128,2,128]{3,2,1,0:T(2,128)}, u32[]{:S(2)}) copy-start(f32[2,128,2,128]{3,2,1,0:T(2,128)} %reduce_sum.77) | copy-start | bytes 786436
  189.0 63.4 %collective-permute-start.9 = (f32[4,2,128,2,128]{4,2,3,1,0:T(8,128)S(1)}, f32[4,2,128,2,128]{4,2,3,1,0:T(8,128)S(1)}, u32[]{:S(2)}, u32[]{:S(2)}) collective-permute-start(f32[4,2,128,2,128]{4,2,3,1,0:T(8,128)S(1)} %pad_maximum_fusion), channel_id=1, source_target_pairs={{0,12},{1,13},{2,14},{3,15},{4,0},{5,1},{6,2},{7,3},{8,4},{9,5},{1... | collective-permute-start | bytes 3145736 | tf_op jit(solution)/shard_map/ppermute | solution.py:26
  190.4 60.9 %collective-permute-start.8 = (f32[4,2,128,2,128]{4,2,3,1,0:T(8,128)S(1)}, f32[4,2,128,2,128]{4,2,3,1,0:T(8,128)S(1)}, u32[]{:S(2)}, u32[]{:S(2)}) collective-permute-start(f32[4,2,128,2,128]{4,2,3,1,0:T(8,128)S(1)} %pad_maximum_fusion), channel_id=1, source_target_pairs={{0,8},{1,9},{2,10},{3,11},{4,12},{5,13},{6,14},{7,15},{8,0},{9,1},... | collective-permute-start | bytes 3145736 | tf_op jit(solution)/shard_map/ppermute | solution.py:26
  271.0 9.3 %copy-start.3 = (f32[4,128,2,128]{3,2,1,0:T(2,128)S(1)}, f32[4,128,2,128]{3,2,1,0:T(2,128)}, u32[]{:S(2)}) copy-start(f32[4,128,2,128]{3,2,1,0:T(2,128)} %get-tuple-element.12) | copy-start | bytes 1572868
  271.0 9.4 %copy-start.12 = (f32[2]{0:T(128)S(1)}, f32[2]{0:T(128)}, u32[]{:S(2)}) copy-start(f32[2]{0:T(128)} %copy-done.11) | copy-start | bytes 28
  286.6 38.0 %copy-start.2 = (f32[4,128,2,128]{3,2,1,0:T(2,128)S(1)}, f32[4,128,2,128]{3,2,1,0:T(2,128)}, u32[]{:S(2)}) copy-start(f32[4,128,2,128]{3,2,1,0:T(2,128)} %param.5) | copy-start | bytes 1572868
  (4 other events, 5.9 us)
Sparse Core Ops, SparseCore 0:
  14.1 73.4 all-gather.4
  125.3 33.4 reduce-scatter.2
  166.0 83.8 all-gather.6
  288.6 34.7 reduce-scatter.4
